TPU v7x, 32 devices: a whole 2x2x4 slice. The times are simulated.
32 devices in a mesh: seq: 8 (over z, x), exp: 4 (over y, core).
Axes of the slice: x: 2, y: 2, z: 4, core: 2. Of those that a mesh axis runs over, the one named last changes fastest.
Arguments:
- hidden_in: bfloat16 [2048, 1536], P('seq'), may hold values from -6 to 6
- attn_gain: float32 [1536], replicated, may hold values from 0.1 to 1.9
- q_weight: bfloat16 [1536, 1536], P(None, 'exp'), may hold values from -1.25 to 1.25
- k_weight: bfloat16 [1536, 512], P(None, 'exp'), may hold values from -0.625 to 0.625
- v_weight: bfloat16 [1536, 512], P(None, 'exp'), may hold values from -0.15625 to 0.15625
- o_weight: bfloat16 [1536, 1536], P('exp'), may hold values from -0.15625 to 0.15625
- cache_kv: bfloat16 [4096, 1024], P('seq', 'exp'), may hold values from -216 to 216
- moe_gain: float32 [1536], replicated, may hold values from 0.1 to 1.9
- expert_in: bfloat16 [32, 1536, 1024], P('seq'), may hold values from -0.15625 to 0.15625
- expert_out: bfloat16 [32, 512, 1536], P('seq'), may hold values from -0.25 to 0.25
- routes: int32 [2048, 8], P(('seq', 'exp')), may hold values from 0 to 31, all different within a row; in each aligned block of 64 rows (0 to 63, 64 to 127, ...) at most 32 rows name the same one
- route_prob: float32 [2048, 8], P(('seq', 'exp')), may hold values from 0.05 to 1
- page_slot: int32 [256], replicated, may hold values from 0 to 31, as said below
Outputs:
- hidden_out: bfloat16 [2048, 1536], P(('seq', 'exp'))
- decode_pages: bfloat16 [256, 8, 2, 512], P('seq', 'exp')
Inputs may be any that keep to these rules, and one draw needn't show every extreme that they name: `routes`: in each aligned block of 64 rows (the rows of one device) no expert is named by more than 32 rows; a row names 8 different experts. `page_slot`: for each r, the 32 blocks b with b mod (8) == r have different slots.
All inputs are finite; a program needn't handle non-finite values.
Results may differ from a plain program's by a relative error of at most 0.0074.
Values may be sent and summed in bfloat16 or wider, within the bound.
No kernel may reach another device: no remote copies, remote signals or barrier semaphores. Data moves between devices by JAX's collectives and lax.ppermute only.
A program may use at most 128 MiB of HBM per device.

v0:
```python
import math
import jax
import jax.numpy as jnp
from jax import lax
from jax.sharding import PartitionSpec as P

HEADS = 24
KV_HEADS = 8
HEAD_DIM = 64
EXPERTS = 32
PAGE = 8
norm_epsilon = 1e-06
attention_scale = 0.015625
residual_scale = 0.22
masked_score = -1e30


def rms_norm(values, gain_row):
    widened = values.astype(jnp.float32)
    spread = lax.rsqrt(jnp.mean(widened * widened, axis=-1, keepdims=True) + norm_epsilon)
    return (widened * spread * gain_row).astype(jnp.bfloat16)


def attend_block(carried, query_heads, visible, key_rows, value_rows):
    best_old, total_old, summed_old = carried
    scores = (
        jnp.einsum("tkgd,nkd->kgtn", query_heads, key_rows, preferred_element_type=jnp.float32)
        * attention_scale
    )
    scores = jnp.where(visible, scores, masked_score)
    best_new = jnp.maximum(best_old, jnp.max(scores, axis=-1))
    weights = jnp.where(visible, jnp.exp(scores - best_new[..., None]), 0.0)
    factor = jnp.exp(best_old - best_new)
    total_new = total_old * factor + jnp.sum(weights, axis=-1)
    summed_new = summed_old * factor[..., None] + jnp.einsum(
        "kgtn,nkd->kgtd",
        weights.astype(jnp.bfloat16),
        value_rows,
        preferred_element_type=jnp.float32,
    )
    return (best_new, total_new, summed_new)


def block_size(piece_rows):
    return math.gcd(piece_rows, 512)


def body(
    hidden_in,
    attn_gain,
    q_weight,
    k_weight,
    v_weight,
    o_weight,
    cache_kv,
    moe_gain,
    expert_in,
    expert_out,
    routes,
    route_prob,
    page_slot,
):
    seq_count = lax.axis_size("seq")
    seq_index = lax.axis_index("seq")
    exp_index = lax.axis_index("exp")
    tokens_here = hidden_in.shape[0]
    head_dim = HEAD_DIM
    kv_local = k_weight.shape[1] // head_dim
    group_size = HEADS // KV_HEADS
    prompt_len = tokens_here * seq_count // 2
    first_row = seq_index * tokens_here
    query_rows = first_row + jnp.arange(tokens_here, dtype=jnp.int32)
    query_second = query_rows >= prompt_len
    holds_first = first_row < prompt_len
    normed = rms_norm(hidden_in, attn_gain)
    queries = jnp.dot(normed, q_weight, preferred_element_type=jnp.float32).astype(jnp.bfloat16)
    keys_new = jnp.dot(normed, k_weight, preferred_element_type=jnp.float32).astype(jnp.bfloat16)
    values_new = jnp.dot(normed, v_weight, preferred_element_type=jnp.float32).astype(jnp.bfloat16)
    pair_width = 2 * kv_local * head_dim
    pairs_new = jnp.stack(
        [
            keys_new.reshape(tokens_here, kv_local, head_dim),
            values_new.reshape(tokens_here, kv_local, head_dim),
        ],
        axis=2,
    ).reshape(tokens_here, pair_width)
    query_heads = queries.reshape(tokens_here, kv_local, group_size, head_dim)
    cache_lines = cache_kv.reshape(tokens_here, -1)
    blocks_here = tokens_here // PAGE
    rounds = blocks_here // seq_count
    outgoing = pairs_new.reshape(rounds, seq_count, PAGE * pair_width)
    received = lax.all_to_all(outgoing, "seq", split_axis=1, concat_axis=1, tiled=True)
    block_ids = (
        jnp.arange(seq_count, dtype=jnp.int32)[None, :] * blocks_here
        + jnp.arange(rounds, dtype=jnp.int32)[:, None] * seq_count
        + seq_index
    ).reshape(-1)
    table_ids = jnp.arange(page_slot.shape[0], dtype=jnp.int32)
    page_slots = jnp.sum(
        jnp.where(block_ids[:, None] == table_ids[None, :], page_slot[None, :], 0), axis=1
    )
    local_pages = (
        jnp.zeros((blocks_here, PAGE * pair_width), jnp.bfloat16)
        .at[page_slots]
        .set(received.reshape(blocks_here, -1))
    )
    page_rows = local_pages.reshape(blocks_here, PAGE, kv_local, 2, head_dim).transpose(
        0, 2, 3, 1, 4
    )
    page_rows = page_rows.reshape(blocks_here, kv_local, 2, PAGE * head_dim)
    start_state = (
        jnp.full((kv_local, group_size, tokens_here), masked_score, jnp.float32),
        jnp.zeros((kv_local, group_size, tokens_here), jnp.float32),
        jnp.zeros((kv_local, group_size, tokens_here, head_dim), jnp.float32),
    )

    def new_keys_part(carried, new_block, key_first):
        width_rows = new_block.shape[0]
        key_rows = key_first + jnp.arange(width_rows, dtype=jnp.int32)
        visible = ((key_rows >= prompt_len)[None, :] == query_second[:, None]) & (
            key_rows[None, :] <= query_rows[:, None]
        )
        split_pairs = new_block.reshape(width_rows, kv_local, 2, head_dim)
        return lax.cond(
            jnp.any(visible),
            lambda carried_in: attend_block(
                carried_in, query_heads, visible, split_pairs[:, :, 0], split_pairs[:, :, 1]
            ),
            lambda carried_in: carried_in,
            carried,
        )

    carried = start_state
    new_piece = lax.all_gather(pairs_new, "seq", axis=0, tiled=True)
    cache_piece = lax.all_gather(cache_lines, "seq", axis=0, tiled=True)
    piece_rows = new_piece.shape[0]
    stride = block_size(piece_rows)
    new_blocks = new_piece.reshape(piece_rows // stride, stride, -1)
    cache_blocks = cache_piece.reshape(piece_rows // stride, 2 * stride, kv_local, 2, head_dim)
    offsets = stride * jnp.arange(piece_rows // stride, dtype=jnp.int32)
    everything = jnp.ones((tokens_here, 2 * stride), bool)

    def visit(carried_in, block_part):
        new_block, cache_block, key_first = block_part
        carried_in = new_keys_part(carried_in, new_block, key_first)
        carried_in = lax.cond(
            holds_first,
            lambda inner: attend_block(
                inner, query_heads, everything, cache_block[:, :, 0], cache_block[:, :, 1]
            ),
            lambda inner: inner,
            carried_in,
        )
        return (carried_in, None)

    carried, _ = lax.scan(visit, carried, (new_blocks, cache_blocks, offsets))
    best_final, total_final, summed_final = carried
    attended = (
        (summed_final / total_final[..., None])
        .transpose(2, 0, 1, 3)
        .reshape(tokens_here, -1)
        .astype(jnp.bfloat16)
    )
    mixed_rows = lax.psum_scatter(
        jnp.dot(attended, o_weight, preferred_element_type=jnp.float32).astype(jnp.bfloat16),
        "exp",
        scatter_dimension=0,
        tiled=True,
    ).astype(jnp.float32)
    moe_rows = mixed_rows.shape[0]
    residual = (
        lax.dynamic_slice_in_dim(hidden_in, exp_index * moe_rows, moe_rows, 0).astype(jnp.float32)
        + residual_scale * mixed_rows
    )
    moe_in = rms_norm(residual, moe_gain)
    top_count = routes.shape[1]
    assigns = moe_rows * top_count
    capacity = 2 * moe_rows * top_count // EXPERTS
    flat_ids = routes.reshape(-1)
    hit_table = (flat_ids[:, None] == jnp.arange(EXPERTS, dtype=jnp.int32)[None, :]).astype(
        jnp.int32
    )
    earlier = jnp.cumsum(hit_table, axis=0) - hit_table
    slot_rank = jnp.sum(earlier * hit_table, axis=1)
    dest_slot = flat_ids * capacity + slot_rank
    source = (
        jnp.full((EXPERTS * capacity,), assigns, jnp.int32)
        .at[dest_slot]
        .set(jnp.arange(assigns, dtype=jnp.int32))
    )
    filled = source < assigns
    picked = moe_in[jnp.minimum(source, assigns - 1) // top_count]
    dispatched = jnp.where(filled[:, None], picked, jnp.zeros_like(picked)).reshape(
        seq_count, EXPERTS // seq_count, capacity, -1
    )
    hidden = jnp.einsum(
        "sexd,edf->sexf",
        lax.all_to_all(dispatched, "seq", split_axis=0, concat_axis=0, tiled=True),
        expert_in,
        preferred_element_type=jnp.float32,
    )
    half_width = hidden.shape[-1] // 2
    active = (jax.nn.silu(hidden[..., :half_width]) * hidden[..., half_width:]).astype(jnp.bfloat16)
    produced = jnp.einsum(
        "sexf,efd->sexd", active, expert_out, preferred_element_type=jnp.float32
    ).astype(jnp.bfloat16)
    returned = lax.all_to_all(produced, "seq", split_axis=0, concat_axis=0, tiled=True)
    flat_back = returned.reshape(EXPERTS * capacity, -1)
    per_assign = flat_back[dest_slot].reshape(moe_rows, top_count, -1)
    share = route_prob / jnp.sum(route_prob, axis=-1, keepdims=True)
    moe = jnp.sum(share[..., None] * per_assign.astype(jnp.float32), axis=1)
    hidden_out = (residual + residual_scale * moe).astype(jnp.bfloat16)
    return (hidden_out, page_rows)


def solution(mesh):
    return jax.shard_map(
        body,
        mesh=mesh,
        in_specs=(
            P("seq", None),
            P(),
            P(None, "exp"),
            P(None, "exp"),
            P(None, "exp"),
            P("exp", None),
            P("seq", "exp"),
            P(),
            P("seq", None, None),
            P("seq", None, None),
            P(("seq", "exp"), None),
            P(("seq", "exp"), None),
            P(),
        ),
        out_specs=(P(("seq", "exp"), None), P("seq", "exp", None, None)),
        check_vma=False,
    )
```

profile of v0, /device:TPU:0, one launch (start us, length us, event | category | flops | bytes accessed | tf_op | source)
XLA Modules:
  0.0 385.0 jit_solution(13722507623709581729)
XLA Ops:
  14.7 40.6 %all-gather.3.cloned.1.call-done = bf16[2048,256]{0,1:T(8,128)(2,1)} async-done(((bf16[256,256]{0,1:T(8,128)(2,1)}), bf16[2048,256]{0,1:T(8,128)(2,1)}) %all-gather.3.cloned.1.call-update) | async-done | bytes 1048592 | tf_op jit(solution)/shard_map/all_gather | solution.py:134
  56.7 49.0 %all-gather.5.cloned.1.call-done = bf16[2048,512]{1,0:T(8,128)(2,1)} async-done(((bf16[256,512]{1,0:T(8,128)(2,1)}), bf16[2048,512]{1,0:T(8,128)(2,1)}) %all-gather.5.cloned.1.call-update) | async-done | bytes 2097168 | tf_op jit(solution)/shard_map/all_gather | solution.py:135
  105.7 8.9 %reshape.173 = bf16[4,1024,2,2,64]{4,3,2,1,0:T(2,128)(2,1)} reshape(bf16[2048,512]{1,0:T(8,128)(2,1)} %all-gather.5.cloned.1.call-done) | data formatting | bytes 4194304 | tf_op jit(solution)/shard_map/reshape | solution.py:139
  114.6 10.6 %copy.101 = bf16[4,1024,2,2,64]{1,4,2,3,0:T(8,128)(2,1)} copy(bf16[4,1024,2,2,64]{4,3,2,1,0:T(2,128)(2,1)} %reshape.173) | data formatting | bytes 4194304
  125.3 35.4 %while.16 = (s32[]{:T(128)}, f32[2,3,256]{2,1,0:T(4,128)S(1)}, f32[2,3,256]{2,1,0:T(4,128)S(1)}, f32[2,3,256,64]{2,3,1,0:T(8,128)S(1)}, pred[]{:T(512)}, /*index...) while((s32[]{:T(128)}, f32[2,3,256]{2,1,0:T(4,128)S(1)}, ...), condition=%wide.region_11.12_spmd.clone.clone, body=%wide.region_1.11_spmd.clone.clone.sunk | while | flops 627712256 | bytes 33374036 | solution.py:156
  129.0 2.5 conditional.8
  131.5 4.5 %conditional.9 = ((f32[2,3,256]{2,1,0:T(4,128)S(1)}, f32[2,3,256]{2,1,0:T(4,128)S(1)}, f32[2,3,256,64]{2,3,1,0:T(8,128)S(1)})) conditional(s32[]{:T(128)} %convert_element_type.152, (f32[2,3,256]{2,1,0:T(4,128)S(1)}, f32[2,3,256]{2,1,0:T(4,128)S(1)}, f32[2,3,256,64]{2,3,1,0:T(8,128)S(1)}) %get-tuple-element.445, ...), branch_computations={%region_7.7_spmd, %region_8.10_spmd} | conditional | flops 415435776 | bytes 21532708 | solution.py:146
  139.7 4.5 %conditional.9 = ((f32[2,3,256]{2,1,0:T(4,128)S(1)}, f32[2,3,256]{2,1,0:T(4,128)S(1)}, f32[2,3,256,64]{2,3,1,0:T(8,128)S(1)})) conditional(s32[]{:T(128)} %convert_element_type.152, (f32[2,3,256]{2,1,0:T(4,128)S(1)}, f32[2,3,256]{2,1,0:T(4,128)S(1)}, f32[2,3,256,64]{2,3,1,0:T(8,128)S(1)}) %get-tuple-element.445, ...), branch_computations={%region_7.7_spmd, %region_8.10_spmd} | conditional | flops 415435776 | bytes 21532708 | solution.py:146
  148.0 4.5 %conditional.9 = ((f32[2,3,256]{2,1,0:T(4,128)S(1)}, f32[2,3,256]{2,1,0:T(4,128)S(1)}, f32[2,3,256,64]{2,3,1,0:T(8,128)S(1)})) conditional(s32[]{:T(128)} %convert_element_type.152, (f32[2,3,256]{2,1,0:T(4,128)S(1)}, f32[2,3,256]{2,1,0:T(4,128)S(1)}, f32[2,3,256,64]{2,3,1,0:T(8,128)S(1)}) %get-tuple-element.445, ...), branch_computations={%region_7.7_spmd, %region_8.10_spmd} | conditional | flops 415435776 | bytes 21532708 | solution.py:146
  156.2 4.5 %conditional.9 = ((f32[2,3,256]{2,1,0:T(4,128)S(1)}, f32[2,3,256]{2,1,0:T(4,128)S(1)}, f32[2,3,256,64]{2,3,1,0:T(8,128)S(1)})) conditional(s32[]{:T(128)} %convert_element_type.152, (f32[2,3,256]{2,1,0:T(4,128)S(1)}, f32[2,3,256]{2,1,0:T(4,128)S(1)}, f32[2,3,256,64]{2,3,1,0:T(8,128)S(1)}) %get-tuple-element.445, ...), branch_computations={%region_7.7_spmd, %region_8.10_spmd} | conditional | flops 415435776 | bytes 21532708 | solution.py:146
  164.3 2.4 scatter_custom_fusion
  166.9 19.4 %reduce-scatter.2.cloned.1.call-done = bf16[64,1536]{1,0:T(8,128)(2,1)} async-done(((bf16[256,1536]{1,0:T(8,128)(2,1)}), bf16[64,1536]{1,0:T(8,128)(2,1)}) %reduce-scatter.2.cloned.1.call-update) | async-done | bytes 196624 | tf_op jit(solution)/shard_map/reduce_scatter | solution.py:164
  188.5 5.6 %gather_fusion = bf16[1024,1536]{1,0:T(8,128)(2,1)} fusion(bf16[64,1536]{1,0:T(8,128)(2,1)S(1)} %multiply_convert_fusion, s32[1024]{0:T(1024)S(1)} %fusion.59), kind=kCustom, calls=%fused_computation | custom fusion | bytes 6295552 | tf_op jit(solution)/shard_map/gather | solution.py:192
  194.1 3.8 broadcast_select_fusion
  197.9 5.8 %all-to-all-start = ((bf16[8,4,32,1536]{3,2,1,0:T(8,128)(2,1)}), bf16[8,4,32,1536]{3,2,1,0:T(8,128)(2,1)}, u32[]{:S(2)}, u32[]{:S(2)}) async-start(bf16[8,4,32,1536]{3,2,1,0:T(8,128)(2,1)} %broadcast_select_fusion), calls=%async_computation.1 | async-start | bytes 6291456 | tf_op jit(solution)/shard_map/all_to_all | solution.py:198
  204.9 69.6 %all-to-all-done = bf16[8,4,32,1536]{3,2,1,0:T(8,128)(2,1)} async-done(((bf16[8,4,32,1536]{3,2,1,0:T(8,128)(2,1)}), bf16[8,4,32,1536]{3,2,1,0:T(8,128)(2,1)}, u32[]{:S(2)}, u32[]{:S(2)}) %all-to-all-start) | async-done | bytes 3145760 | tf_op jit(solution)/shard_map/all_to_all | solution.py:198
  274.5 3.6 all-to-all-start.2
  278.2 7.4 %fusion.39 = f32[8,4,32,1024]{3,2,0,1:T(8,128)S(1)} fusion(bf16[4,1536,1024]{2,1,0:T(8,128)(2,1)} %param.27, bf16[8,4,32,1536]{3,2,1,0:T(8,128)(2,1)} %all-to-all-done), kind=kOutput, calls=%fused_computation.53 | convolution fusion | flops 3221225472 | bytes 19922944 | tf_op jit(solution)/shard_map/sexd,edf->sexf/dot_general | solution.py:196
  285.6 4.6 %fusion.34 = bf16[8,4,32,1536]{3,2,0,1:T(8,128)(2,1)S(1)} fusion(bf16[4,512,1536]{2,1,0:T(8,128)(2,1)} %param.28, f32[8,4,32,1024]{3,2,0,1:T(8,128)S(1)} %fusion.39), kind=kOutput, calls=%fused_computation.47 | convolution fusion | flops 1615331328 | bytes 13631488 | tf_op jit(solution)/shard_map/sexf,efd->sexd/dot_general | solution.py:204
  290.2 1.9 copy.108
  292.1 6.1 %all-to-all-start.1 = ((bf16[8,4,32,1536]{3,2,1,0:T(8,128)(2,1)}), bf16[8,4,32,1536]{3,2,1,0:T(8,128)(2,1)}, u32[]{:S(2)}, u32[]{:S(2)}) async-start(bf16[8,4,32,1536]{3,2,1,0:T(8,128)(2,1)} %copy.108), calls=%async_computation.2 | async-start | bytes 6291456 | tf_op jit(solution)/shard_map/all_to_all | solution.py:207
  301.4 67.3 %all-to-all-done.1 = bf16[8,4,32,1536]{3,2,1,0:T(8,128)(2,1)} async-done(((bf16[8,4,32,1536]{3,2,1,0:T(8,128)(2,1)}), bf16[8,4,32,1536]{3,2,1,0:T(8,128)(2,1)}, u32[]{:S(2)}, u32[]{:S(2)}) %all-to-all-start.1) | async-done | bytes 3145760 | tf_op jit(solution)/shard_map/all_to_all | solution.py:207
  368.7 5.9 %gather_fusion.1 = bf16[512,1536]{1,0:T(8,128)(2,1)S(1)} fusion(bf16[1024,1536]{1,0:T(8,128)(2,1)} %bitcast.33, s32[1024]{0:T(1024)S(1)} %pad_clamp_fusion), kind=kCustom, calls=%fused_computation.1 | custom fusion | bytes 3147776 | tf_op jit(solution)/shard_map/gather | solution.py:209
  374.6 2.2 fusion.37
  (147 shorter events, 52.7 us)
Async XLA Ops:
  7.2 153.6 %copy-start = (bf16[384,1536]{1,0:T(8,128)(2,1)S(1)}, bf16[384,1536]{1,0:T(8,128)(2,1)}, u32[]{:S(2)}) copy-start(bf16[384,1536]{1,0:T(8,128)(2,1)} %param.24) | copy-start | bytes 3538948
  7.2 6.7 %copy-start.1 = (bf16[256,1536]{1,0:T(8,128)(2,1)S(1)}, bf16[256,1536]{1,0:T(8,128)(2,1)}, u32[]{:S(2)}) copy-start(bf16[256,1536]{1,0:T(8,128)(2,1)} %param.19) | copy-start | bytes 2359300
  7.2 6.7 %copy-start.10 = (f32[1536]{0:T(1024)S(1)}, f32[1536]{0:T(1024)}, u32[]{:S(2)}) copy-start(f32[1536]{0:T(1024)} %param.20) | copy-start | bytes 18436
  7.2 5.8 %copy-start.4 = (bf16[512,256]{1,0:T(8,128)(2,1)S(1)}, bf16[512,256]{1,0:T(8,128)(2,1)}, u32[]{:S(2)}) copy-start(bf16[512,256]{1,0:T(8,128)(2,1)} %param.25) | copy-start | bytes 786436
  7.2 6.7 %copy-start.9 = (bf16[1536,384]{1,0:T(8,128)(2,1)S(1)}, bf16[1536,384]{1,0:T(8,128)(2,1)}, u32[]{:S(2)}) copy-start(bf16[1536,384]{1,0:T(8,128)(2,1)} %param.21) | copy-start | bytes 3538948
  7.2 48.1 %all-gather.3.cloned.1.call-start = ((), (), s32[]{:S(2)}) async-start(), calls=%async_computation.4 | async-start | bytes 1179648 | tf_op jit(solution)/shard_map/all_gather | solution.py:134
  13.0 92.7 %all-gather.5.cloned.1.call-start = ((), (), s32[]{:S(2)}) async-start(), calls=%async_computation.5 | async-start | bytes 2359296 | tf_op jit(solution)/shard_map/all_gather | solution.py:135
  13.9 172.4 %reduce-scatter.2.cloned.1.call-start = ((), (), s32[]{:S(2)}) async-start(), calls=%async_computation.6 | async-start | bytes 983040 | tf_op jit(solution)/shard_map/reduce_scatter | solution.py:164
  160.7 1.6 copy-start.5
  160.7 25.6 %copy-start.2 = (bf16[256,1536]{1,0:T(8,128)(2,1)S(1)}, bf16[256,1536]{1,0:T(8,128)(2,1)}, u32[]{:S(2)}) copy-start(bf16[256,1536]{1,0:T(8,128)(2,1)} %param.19) | copy-start | bytes 2359300
  160.7 26.7 %copy-start.7 = (f32[1536]{0:T(1024)S(1)}, f32[1536]{0:T(1024)}, u32[]{:S(2)}) copy-start(f32[1536]{0:T(1024)} %param.26) | copy-start | bytes 18436
  197.9 5.8 %copy-start.3 = (bf16[256,2,2,64]{0,3,2,1:T(8,128)(2,1)S(1)}, bf16[256,2,2,64]{0,3,2,1:T(8,128)(2,1)}, u32[]{:S(2)}) copy-start(bf16[256,2,2,64]{0,3,2,1:T(8,128)(2,1)} %pad_maximum_fusion) | copy-start | bytes 393220
  197.9 76.6 %all-to-all-start = ((bf16[8,4,32,1536]{3,2,1,0:T(8,128)(2,1)}), bf16[8,4,32,1536]{3,2,1,0:T(8,128)(2,1)}, u32[]{:S(2)}, u32[]{:S(2)}) async-start(bf16[8,4,32,1536]{3,2,1,0:T(8,128)(2,1)} %broadcast_select_fusion), calls=%async_computation.1 | async-start | bytes 6291456 | tf_op jit(solution)/shard_map/all_to_all | solution.py:198
  274.5 17.6 %all-to-all-start.2 = ((bf16[4,8,2048]{2,0,1:T(4,128)(2,1)}), bf16[4,8,2048]{2,0,1:T(4,128)(2,1)S(1)}, u32[]{:S(2)}, u32[]{:S(2)}) async-start(bf16[4,8,2048]{2,0,1:T(4,128)(2,1)} %copy.110), calls=%async_computation.3 | async-start | bytes 262144 | tf_op jit(solution)/shard_map/all_to_all | solution.py:92
  292.1 6.1 %copy-start.6 = (f32[64,8]{0,1:T(8,128)S(1)}, f32[64,8]{0,1:T(8,128)}, u32[]{:S(2)}) copy-start(f32[64,8]{0,1:T(8,128)} %param.30) | copy-start | bytes 6148
  292.1 7.1 %copy-start.8 = (s32[256]{0:T(256)S(1)}, s32[256]{0:T(256)}, u32[]{:S(2)}) copy-start(s32[256]{0:T(256)} %param.31) | copy-start | bytes 3076
  292.1 76.6 %all-to-all-start.1 = ((bf16[8,4,32,1536]{3,2,1,0:T(8,128)(2,1)}), bf16[8,4,32,1536]{3,2,1,0:T(8,128)(2,1)}, u32[]{:S(2)}, u32[]{:S(2)}) async-start(bf16[8,4,32,1536]{3,2,1,0:T(8,128)(2,1)} %copy.108), calls=%async_computation.2 | async-start | bytes 6291456 | tf_op jit(solution)/shard_map/all_to_all | solution.py:207
Sparse Core Ops, SparseCore 0:
  13.1 42.2 all-gather.2
  57.5 48.1 all-gather.4
  162.4 23.8 reduce-scatter.1
where the time goes:
time: 386 us; the launch traced here: 385 us
  waiting for transfers between devices  246 us (64%)
  local copies, waits for them, and re-layouts  49.6 us (13%)
  matrix products  28.3 us (7%)
  other arithmetic  28.1 us (7%)
  starting transfers between devices  15.7 us (4%)
  between operations  14.1 us (4%)
    all_to_all x1, waiting for transfers between devices, body(): lax.all_to_all(dispatched, 'seq', split_axis=0, concat_axis=0, tiled=True)  69.6 us
    all_to_all x1, waiting for transfers between devices, body(): lax.all_to_all(produced, 'seq', split_axis=0, concat_axis=0, tiled=True)  67.3 us
    all_gather x1, waiting for transfers between devices, body(): cache_piece = lax.all_gather(cache_lines, 'seq', axis=0, tiled=True)  49 us
    all_gather x1, waiting for transfers between devices, body(): new_piece = lax.all_gather(pairs_new, 'seq', axis=0, tiled=True)  40.6 us
    reduce_scatter x1, waiting for transfers between devices, body(): lax.psum_scatter(jnp.dot(attended, o_weight, preferred_element_type=jnp.f...  19.4 us
    unnamed x26, local copies, waits for them, and re-layouts  11.7 us
    reshape x1, local copies, waits for them, and re-layouts, body(): cache_piece.reshape(piece_rows // stride, 2 * stride, kv_local, 2, head_dim)  8.88 us
  transfers between devices with their start and end apart: 6, of which 5 were waited for; matrix products, arithmetic and copies ran while one was open for 7% of the time, Pallas kernels for 0%

commit v1 on v0

--- a/solution.py
+++ b/solution.py
@@ -13,6 +13,12 @@
 attention_scale = 0.015625
 residual_scale = 0.22
 masked_score = -1e30
+
+
+def in_order(tiles, dim):
+    tiles = jnp.moveaxis(tiles, 0, dim)
+    shape = tiles.shape
+    return tiles.reshape(*shape[:dim], shape[dim] * shape[dim + 1], *shape[dim + 2 :])
 
 
 def rms_norm(values, gain_row):
@@ -132,7 +138,14 @@
 
     carried = start_state
     new_piece = lax.all_gather(pairs_new, "seq", axis=0, tiled=True)
-    cache_piece = lax.all_gather(cache_lines, "seq", axis=0, tiled=True)
+    devices = lax.axis_size("seq")
+    right = [(i, (i + 1) % devices) for i in range(devices)]
+    tiles = [cache_lines]
+    while len(tiles) < devices:
+        tiles.append(lax.ppermute(tiles[-1], "seq", right))
+    index = lax.axis_index("seq")
+    tiles = jnp.stack(tiles)[(index - jnp.arange(devices)) % devices]
+    cache_piece = in_order(tiles, 0)
     piece_rows = new_piece.shape[0]
     stride = block_size(piece_rows)
     new_blocks = new_piece.reshape(piece_rows // stride, stride, -1)

time: 386 us -> 358 us (0.927)
  waiting for transfers between devices: 246 us -> 212 us
    ppermute x0 -> x7, waiting for transfers between devices: none -> 59 us  [body(): tiles.append(lax.ppermute(tiles[-1], 'seq', right))]
    all_gather x1 -> x0, waiting for transfers between devices: 49 us -> none  [body(): cache_piece = lax.all_gather(cache_lines, 'seq', axis=0, tiled=True)]
    all_gather x1, waiting for transfers between devices: 40.6 us -> 0.01 us  [body(): new_piece = lax.all_gather(pairs_new, 'seq', axis=0, tiled=True)]
    reshape x1 -> x0, local copies, waits for them, and re-layouts: 8.88 us -> none  [body(): cache_piece.reshape(piece_rows // stride, 2 * stride, kv_local, 2, head_dim)]
    unnamed x26 -> x31, local copies, waits for them, and re-layouts: 11.7 us -> 16.7 us
    another operation x1 -> x4, local copies, waits for them, and re-layouts: 0.01 us -> 4.48 us  [the longest x1 3.66 us: body(): cache_piece.reshape(piece_rows // stride, 2 * stride, kv_local, 2, head_dim)]
  transfers between devices with their start and end apart: 6 -> 12, of which waited for: 5 -> 10; matrix products, arithmetic and copies ran while one was open for 7% -> 15% of each run, Pallas kernels for 0% -> 0%
where the time goes in v1:
time: 358 us; the launch traced here: 356 us
  waiting for transfers between devices  212 us (59%)
  local copies, waits for them, and re-layouts  52.7 us (15%)
  matrix products  29.6 us (8%)
  other arithmetic  26.7 us (7%)
  starting transfers between devices  18.5 us (5%)
  between operations  14.4 us (4%)
    all_to_all x1, waiting for transfers between devices, body(): lax.all_to_all(dispatched, 'seq', split_axis=0, concat_axis=0, tiled=True)  69.6 us
    all_to_all x1, waiting for transfers between devices, body(): lax.all_to_all(produced, 'seq', split_axis=0, concat_axis=0, tiled=True)  67.3 us
    ppermute x7, waiting for transfers between devices, body(): tiles.append(lax.ppermute(tiles[-1], 'seq', right))  59 us
    unnamed x31, local copies, waits for them, and re-layouts  16.7 us
    reduce_scatter x1, waiting for transfers between devices, body(): lax.psum_scatter(jnp.dot(attended, o_weight, preferred_element_type=jnp.f...  15.8 us
    dot_general x1, matrix products, body(): jnp.einsum('sexd,edf->sexf', lax.all_to_all(dispatched, 'seq', split_axis...  7.37 us
  transfers between devices with their start and end apart: 12, of which 10 were waited for; matrix products, arithmetic and copies ran while one was open for 15% of the time, Pallas kernels for 0%

profile of v1, /device:TPU:0, one launch (start us, length us, event | category | flops | bytes accessed | tf_op | source)
XLA Modules:
  0.0 356.5 jit_solution(16678271732345256377)
XLA Ops:
  14.6 6.2 %collective-permute-done = bf16[256,512]{1,0:T(8,128)(2,1)S(1)} collective-permute-done((bf16[256,512]{1,0:T(8,128)(2,1)S(1)}, bf16[256,512]{1,0:T(8,128)(2,1)S(1)}, u32[]{:S(2)}, u32[]{:S(2)}) %collective-permute-start) | collective-permute-done | bytes 262176 | tf_op jit(solution)/shard_map/ppermute | solution.py:145
  23.3 7.7 %collective-permute-done.1 = bf16[256,512]{1,0:T(8,128)(2,1)S(1)} collective-permute-done((bf16[256,512]{1,0:T(8,128)(2,1)S(1)}, bf16[256,512]{1,0:T(8,128)(2,1)S(1)}, u32[]{:S(2)}, u32[]{:S(2)}) %collective-permute-start.1) | collective-permute-done | bytes 262176 | tf_op jit(solution)/shard_map/ppermute | solution.py:145
  32.9 8.9 %collective-permute-done.2 = bf16[256,512]{1,0:T(8,128)(2,1)S(1)} collective-permute-done((bf16[256,512]{1,0:T(8,128)(2,1)S(1)}, bf16[256,512]{1,0:T(8,128)(2,1)S(1)}, u32[]{:S(2)}, u32[]{:S(2)}) %collective-permute-start.2) | collective-permute-done | bytes 262176 | tf_op jit(solution)/shard_map/ppermute | solution.py:145
  42.8 8.1 %collective-permute-done.3 = bf16[256,512]{1,0:T(8,128)(2,1)S(1)} collective-permute-done((bf16[256,512]{1,0:T(8,128)(2,1)S(1)}, bf16[256,512]{1,0:T(8,128)(2,1)S(1)}, u32[]{:S(2)}, u32[]{:S(2)}) %collective-permute-start.3) | collective-permute-done | bytes 262176 | tf_op jit(solution)/shard_map/ppermute | solution.py:145
  52.3 13.0 %collective-permute-done.4 = bf16[256,512]{1,0:T(8,128)(2,1)S(1)} collective-permute-done((bf16[256,512]{1,0:T(8,128)(2,1)S(1)}, bf16[256,512]{1,0:T(8,128)(2,1)S(1)}, u32[]{:S(2)}, u32[]{:S(2)}) %collective-permute-start.4) | collective-permute-done | bytes 262176 | tf_op jit(solution)/shard_map/ppermute | solution.py:145
  66.7 7.6 %collective-permute-done.5 = bf16[256,512]{1,0:T(8,128)(2,1)S(1)} collective-permute-done((bf16[256,512]{1,0:T(8,128)(2,1)S(1)}, bf16[256,512]{1,0:T(8,128)(2,1)S(1)}, u32[]{:S(2)}, u32[]{:S(2)}) %collective-permute-start.5) | collective-permute-done | bytes 262176 | tf_op jit(solution)/shard_map/ppermute | solution.py:145
  75.8 7.6 %collective-permute-done.6 = bf16[256,512]{1,0:T(8,128)(2,1)S(1)} collective-permute-done((bf16[256,512]{1,0:T(8,128)(2,1)S(1)}, bf16[256,512]{1,0:T(8,128)(2,1)S(1)}, u32[]{:S(2)}, u32[]{:S(2)}) %collective-permute-start.6) | collective-permute-done | bytes 262176 | tf_op jit(solution)/shard_map/ppermute | solution.py:145
  86.4 3.7 %reshape_reshape.6 = bf16[4,1024,2,2,64]{4,3,2,1,0:T(2,128)(2,1)} reshape(bf16[8,256,512]{2,1,0:T(8,128)(2,1)S(1)} %gather_fusion) | data formatting | bytes 4194304 | tf_op jit(solution)/shard_map/reshape;reshape | solution.py:152
  90.0 10.6 %copy.101 = bf16[4,1024,2,2,64]{1,4,2,3,0:T(8,128)(2,1)} copy(bf16[4,1024,2,2,64]{4,3,2,1,0:T(2,128)(2,1)} %reshape_reshape.6) | data formatting | bytes 4194304
  102.1 33.4 %while.16 = (s32[]{:T(128)}, f32[2,3,256]{2,1,0:T(4,128)S(1)}, f32[2,3,256]{2,1,0:T(4,128)S(1)}, f32[2,3,256,64]{2,3,1,0:T(8,128)S(1)}, pred[]{:T(512)}, /*index...) while((s32[]{:T(128)}, f32[2,3,256]{2,1,0:T(4,128)S(1)}, ...), condition=%wide.region_11.12_spmd.clone.clone, body=%wide.region_1.11_spmd.clone.clone.sunk | while | flops 627712256 | bytes 33374036 | solution.py:169
  107.8 4.5 %conditional.9 = ((f32[2,3,256]{2,1,0:T(4,128)S(1)}, f32[2,3,256]{2,1,0:T(4,128)S(1)}, f32[2,3,256,64]{2,3,1,0:T(8,128)S(1)})) conditional(s32[]{:T(128)} %convert_element_type.152, (f32[2,3,256]{2,1,0:T(4,128)S(1)}, f32[2,3,256]{2,1,0:T(4,128)S(1)}, f32[2,3,256,64]{2,3,1,0:T(8,128)S(1)}) %get-tuple-element.445, ...), branch_computations={%region_7.7_spmd, %region_8.10_spmd} | conditional | flops 415435776 | bytes 21532708 | solution.py:159
  115.5 4.5 %conditional.9 = ((f32[2,3,256]{2,1,0:T(4,128)S(1)}, f32[2,3,256]{2,1,0:T(4,128)S(1)}, f32[2,3,256,64]{2,3,1,0:T(8,128)S(1)})) conditional(s32[]{:T(128)} %convert_element_type.152, (f32[2,3,256]{2,1,0:T(4,128)S(1)}, f32[2,3,256]{2,1,0:T(4,128)S(1)}, f32[2,3,256,64]{2,3,1,0:T(8,128)S(1)}) %get-tuple-element.445, ...), branch_computations={%region_7.7_spmd, %region_8.10_spmd} | conditional | flops 415435776 | bytes 21532708 | solution.py:159
  123.3 4.5 %conditional.9 = ((f32[2,3,256]{2,1,0:T(4,128)S(1)}, f32[2,3,256]{2,1,0:T(4,128)S(1)}, f32[2,3,256,64]{2,3,1,0:T(8,128)S(1)})) conditional(s32[]{:T(128)} %convert_element_type.152, (f32[2,3,256]{2,1,0:T(4,128)S(1)}, f32[2,3,256]{2,1,0:T(4,128)S(1)}, f32[2,3,256,64]{2,3,1,0:T(8,128)S(1)}) %get-tuple-element.445, ...), branch_computations={%region_7.7_spmd, %region_8.10_spmd} | conditional | flops 415435776 | bytes 21532708 | solution.py:159
  131.0 4.5 %conditional.9 = ((f32[2,3,256]{2,1,0:T(4,128)S(1)}, f32[2,3,256]{2,1,0:T(4,128)S(1)}, f32[2,3,256,64]{2,3,1,0:T(8,128)S(1)})) conditional(s32[]{:T(128)} %convert_element_type.152, (f32[2,3,256]{2,1,0:T(4,128)S(1)}, f32[2,3,256]{2,1,0:T(4,128)S(1)}, f32[2,3,256,64]{2,3,1,0:T(8,128)S(1)}) %get-tuple-element.445, ...), branch_computations={%region_7.7_spmd, %region_8.10_spmd} | conditional | flops 415435776 | bytes 21532708 | solution.py:159
  141.9 15.8 %reduce-scatter.2.cloned.1.call-done = bf16[64,1536]{1,0:T(8,128)(2,1)} async-done(((bf16[256,1536]{1,0:T(8,128)(2,1)}), bf16[64,1536]{1,0:T(8,128)(2,1)}) %reduce-scatter.2.cloned.1.call-update) | async-done | bytes 196624 | tf_op jit(solution)/shard_map/reduce_scatter | solution.py:177
  159.8 5.6 %gather_fusion.1 = bf16[1024,1536]{1,0:T(8,128)(2,1)} fusion(bf16[64,1536]{1,0:T(8,128)(2,1)S(1)} %multiply_convert_fusion, s32[1024]{0:T(1024)S(1)} %fusion.59), kind=kCustom, calls=%fused_computation.1 | custom fusion | bytes 6295552 | tf_op jit(solution)/shard_map/gather | solution.py:205
  165.4 3.8 %broadcast_select_fusion = bf16[8,4,32,1536]{3,2,1,0:T(8,128)(2,1)} fusion(bf16[8,4,32,1536]{3,2,1,0:T(8,128)(2,1)} %bitcast.157, pred[8,4,32]{2,1,0:T(4,128)(4,1)S(1)} %broadcast_in_dim.87), kind=kLoop, calls=%fused_computation.52 | loop fusion | flops 1572864 | bytes 6292480 | tf_op jit(solution)/shard_map/jit(_where)/select_n | solution.py:206
  169.2 5.6 %all-to-all-start = ((bf16[8,4,32,1536]{3,2,1,0:T(8,128)(2,1)}), bf16[8,4,32,1536]{3,2,1,0:T(8,128)(2,1)}, u32[]{:S(2)}, u32[]{:S(2)}) async-start(bf16[8,4,32,1536]{3,2,1,0:T(8,128)(2,1)} %broadcast_select_fusion), calls=%async_computation.1 | async-start | bytes 6291456 | tf_op jit(solution)/shard_map/all_to_all | solution.py:211
  176.1 69.6 %all-to-all-done = bf16[8,4,32,1536]{3,2,1,0:T(8,128)(2,1)} async-done(((bf16[8,4,32,1536]{3,2,1,0:T(8,128)(2,1)}), bf16[8,4,32,1536]{3,2,1,0:T(8,128)(2,1)}, u32[]{:S(2)}, u32[]{:S(2)}) %all-to-all-start) | async-done | bytes 3145760 | tf_op jit(solution)/shard_map/all_to_all | solution.py:211
  249.3 7.4 %fusion.39 = f32[8,4,32,1024]{3,2,0,1:T(8,128)S(1)} fusion(bf16[4,1536,1024]{2,1,0:T(8,128)(2,1)} %param.27, bf16[8,4,32,1536]{3,2,1,0:T(8,128)(2,1)} %all-to-all-done), kind=kOutput, calls=%fused_computation.54 | convolution fusion | flops 3221225472 | bytes 19922944 | tf_op jit(solution)/shard_map/sexd,edf->sexf/dot_general | solution.py:209
  256.7 4.6 %fusion.34 = bf16[8,4,32,1536]{3,2,0,1:T(8,128)(2,1)S(1)} fusion(bf16[4,512,1536]{2,1,0:T(8,128)(2,1)} %param.28, f32[8,4,32,1024]{3,2,0,1:T(8,128)S(1)} %fusion.39), kind=kOutput, calls=%fused_computation.48 | convolution fusion | flops 1615331328 | bytes 13631488 | tf_op jit(solution)/shard_map/sexf,efd->sexd/dot_general | solution.py:217
  263.3 6.1 %all-to-all-start.1 = ((bf16[8,4,32,1536]{3,2,1,0:T(8,128)(2,1)}), bf16[8,4,32,1536]{3,2,1,0:T(8,128)(2,1)}, u32[]{:S(2)}, u32[]{:S(2)}) async-start(bf16[8,4,32,1536]{3,2,1,0:T(8,128)(2,1)} %copy.108), calls=%async_computation.2 | async-start | bytes 6291456 | tf_op jit(solution)/shard_map/all_to_all | solution.py:220
  272.5 67.3 %all-to-all-done.1 = bf16[8,4,32,1536]{3,2,1,0:T(8,128)(2,1)} async-done(((bf16[8,4,32,1536]{3,2,1,0:T(8,128)(2,1)}), bf16[8,4,32,1536]{3,2,1,0:T(8,128)(2,1)}, u32[]{:S(2)}, u32[]{:S(2)}) %all-to-all-start.1) | async-done | bytes 3145760 | tf_op jit(solution)/shard_map/all_to_all | solution.py:220
  339.8 5.9 %gather_fusion.2 = bf16[512,1536]{1,0:T(8,128)(2,1)S(1)} fusion(bf16[1024,1536]{1,0:T(8,128)(2,1)} %bitcast.41, s32[1024]{0:T(1024)S(1)} %pad_clamp_fusion), kind=kCustom, calls=%fused_computation.2 | custom fusion | bytes 3147776 | tf_op jit(solution)/shard_map/gather | solution.py:222
  (168 shorter events, 76.7 us)
Async XLA Ops:
  7.2 128.4 %copy-start = (bf16[384,1536]{1,0:T(8,128)(2,1)S(1)}, bf16[384,1536]{1,0:T(8,128)(2,1)}, u32[]{:S(2)}) copy-start(bf16[384,1536]{1,0:T(8,128)(2,1)} %param.24) | copy-start | bytes 3538948
  7.2 23.8 %copy-start.1 = (bf16[256,1536]{1,0:T(8,128)(2,1)S(1)}, bf16[256,1536]{1,0:T(8,128)(2,1)}, u32[]{:S(2)}) copy-start(bf16[256,1536]{1,0:T(8,128)(2,1)} %param.19) | copy-start | bytes 2359300
  7.2 23.8 %copy-start.9 = (f32[1536]{0:T(1024)S(1)}, f32[1536]{0:T(1024)}, u32[]{:S(2)}) copy-start(f32[1536]{0:T(1024)} %param.20) | copy-start | bytes 18436
  7.2 93.5 %all-gather.2.cloned.1.call-start = ((), (), s32[]{:S(2)}) async-start(), calls=%async_computation.4 | async-start | bytes 1179648 | tf_op jit(solution)/shard_map/all_gather | solution.py:140
  8.4 12.3 %collective-permute-start = (bf16[256,512]{1,0:T(8,128)(2,1)S(1)}, bf16[256,512]{1,0:T(8,128)(2,1)S(1)}, u32[]{:S(2)}, u32[]{:S(2)}) collective-permute-start(bf16[256,512]{1,0:T(8,128)(2,1)S(1)} %reshape.218), channel_id=1, source_target_pairs={{0,4},{4,8},{8,12},{12,16},{16,20},{20,24},{24,28},{28,0},{1,5},{5... | collective-permute-start | bytes 786440 | tf_op jit(solution)/shard_map/ppermute | solution.py:145
  12.8 29.0 %copy-start.4 = (bf16[512,256]{1,0:T(8,128)(2,1)S(1)}, bf16[512,256]{1,0:T(8,128)(2,1)}, u32[]{:S(2)}) copy-start(bf16[512,256]{1,0:T(8,128)(2,1)} %param.25) | copy-start | bytes 786436
  20.8 10.2 %collective-permute-start.1 = (bf16[256,512]{1,0:T(8,128)(2,1)S(1)}, bf16[256,512]{1,0:T(8,128)(2,1)S(1)}, u32[]{:S(2)}, u32[]{:S(2)}) collective-permute-start(bf16[256,512]{1,0:T(8,128)(2,1)S(1)} %collective-permute-done), channel_id=1, source_target_pairs={{0,4},{4,8},{8,12},{12,16},{16,20},{20,24},{24,28},{28,0},{1,5},{5... | collective-permute-start | bytes 786440 | tf_op jit(solution)/shard_map/ppermute | solution.py:145
  23.2 134.4 %reduce-scatter.2.cloned.1.call-start = ((), (), s32[]{:S(2)}) async-start(), calls=%async_computation.5 | async-start | bytes 983040 | tf_op jit(solution)/shard_map/reduce_scatter | solution.py:177
  30.9 10.8 %collective-permute-start.2 = (bf16[256,512]{1,0:T(8,128)(2,1)S(1)}, bf16[256,512]{1,0:T(8,128)(2,1)S(1)}, u32[]{:S(2)}, u32[]{:S(2)}) collective-permute-start(bf16[256,512]{1,0:T(8,128)(2,1)S(1)} %collective-permute-done.1), channel_id=1, source_target_pairs={{0,4},{4,8},{8,12},{12,16},{16,20},{20,24},{24,28},{28,0},{1,5},{5... | collective-permute-start | bytes 786440 | tf_op jit(solution)/shard_map/ppermute | solution.py:145
  41.8 9.1 %collective-permute-start.3 = (bf16[256,512]{1,0:T(8,128)(2,1)S(1)}, bf16[256,512]{1,0:T(8,128)(2,1)S(1)}, u32[]{:S(2)}, u32[]{:S(2)}) collective-permute-start(bf16[256,512]{1,0:T(8,128)(2,1)S(1)} %collective-permute-done.2), channel_id=1, source_target_pairs={{0,4},{4,8},{8,12},{12,16},{16,20},{20,24},{24,28},{28,0},{1,5},{5... | collective-permute-start | bytes 786440 | tf_op jit(solution)/shard_map/ppermute | solution.py:145
  50.8 14.4 %collective-permute-start.4 = (bf16[256,512]{1,0:T(8,128)(2,1)S(1)}, bf16[256,512]{1,0:T(8,128)(2,1)S(1)}, u32[]{:S(2)}, u32[]{:S(2)}) collective-permute-start(bf16[256,512]{1,0:T(8,128)(2,1)S(1)} %collective-permute-done.3), channel_id=1, source_target_pairs={{0,4},{4,8},{8,12},{12,16},{16,20},{20,24},{24,28},{28,0},{1,5},{5... | collective-permute-start | bytes 786440 | tf_op jit(solution)/shard_map/ppermute | solution.py:145
  65.2 9.1 %collective-permute-start.5 = (bf16[256,512]{1,0:T(8,128)(2,1)S(1)}, bf16[256,512]{1,0:T(8,128)(2,1)S(1)}, u32[]{:S(2)}, u32[]{:S(2)}) collective-permute-start(bf16[256,512]{1,0:T(8,128)(2,1)S(1)} %collective-permute-done.4), channel_id=1, source_target_pairs={{0,4},{4,8},{8,12},{12,16},{16,20},{20,24},{24,28},{28,0},{1,5},{5... | collective-permute-start | bytes 786440 | tf_op jit(solution)/shard_map/ppermute | solution.py:145
  74.3 9.1 %collective-permute-start.6 = (bf16[256,512]{1,0:T(8,128)(2,1)S(1)}, bf16[256,512]{1,0:T(8,128)(2,1)S(1)}, u32[]{:S(2)}, u32[]{:S(2)}) collective-permute-start(bf16[256,512]{1,0:T(8,128)(2,1)S(1)} %collective-permute-done.5), channel_id=1, source_target_pairs={{0,4},{4,8},{8,12},{12,16},{16,20},{20,24},{24,28},{28,0},{1,5},{5... | collective-permute-start | bytes 786440 | tf_op jit(solution)/shard_map/ppermute | solution.py:145
  135.5 1.6 copy-start.5
  135.5 22.1 %copy-start.2 = (bf16[256,1536]{1,0:T(8,128)(2,1)S(1)}, bf16[256,1536]{1,0:T(8,128)(2,1)}, u32[]{:S(2)}) copy-start(bf16[256,1536]{1,0:T(8,128)(2,1)} %param.19) | copy-start | bytes 2359300
  135.5 23.2 %copy-start.7 = (f32[1536]{0:T(1024)S(1)}, f32[1536]{0:T(1024)}, u32[]{:S(2)}) copy-start(f32[1536]{0:T(1024)} %param.26) | copy-start | bytes 18436
  169.2 5.6 %copy-start.3 = (bf16[256,2,2,64]{0,3,2,1:T(8,128)(2,1)S(1)}, bf16[256,2,2,64]{0,3,2,1:T(8,128)(2,1)}, u32[]{:S(2)}) copy-start(bf16[256,2,2,64]{0,3,2,1:T(8,128)(2,1)} %pad_maximum_fusion) | copy-start | bytes 393220
  169.2 76.5 %all-to-all-start = ((bf16[8,4,32,1536]{3,2,1,0:T(8,128)(2,1)}), bf16[8,4,32,1536]{3,2,1,0:T(8,128)(2,1)}, u32[]{:S(2)}, u32[]{:S(2)}) async-start(bf16[8,4,32,1536]{3,2,1,0:T(8,128)(2,1)} %broadcast_select_fusion), calls=%async_computation.1 | async-start | bytes 6291456 | tf_op jit(solution)/shard_map/all_to_all | solution.py:211
  245.7 17.6 %all-to-all-start.2 = ((bf16[4,8,2048]{2,0,1:T(4,128)(2,1)}), bf16[4,8,2048]{2,0,1:T(4,128)(2,1)S(1)}, u32[]{:S(2)}, u32[]{:S(2)}) async-start(bf16[4,8,2048]{2,0,1:T(4,128)(2,1)} %copy.110), calls=%async_computation.3 | async-start | bytes 262144 | tf_op jit(solution)/shard_map/all_to_all | solution.py:98
  263.3 6.1 %copy-start.6 = (f32[64,8]{0,1:T(8,128)S(1)}, f32[64,8]{0,1:T(8,128)}, u32[]{:S(2)}) copy-start(f32[64,8]{0,1:T(8,128)} %param.30) | copy-start | bytes 6148
  263.3 7.0 %copy-start.8 = (s32[256]{0:T(256)S(1)}, s32[256]{0:T(256)}, u32[]{:S(2)}) copy-start(s32[256]{0:T(256)} %param.31) | copy-start | bytes 3076
  263.3 76.6 %all-to-all-start.1 = ((bf16[8,4,32,1536]{3,2,1,0:T(8,128)(2,1)}), bf16[8,4,32,1536]{3,2,1,0:T(8,128)(2,1)}, u32[]{:S(2)}, u32[]{:S(2)}) async-start(bf16[8,4,32,1536]{3,2,1,0:T(8,128)(2,1)} %copy.108), calls=%async_computation.2 | async-start | bytes 6291456 | tf_op jit(solution)/shard_map/all_to_all | solution.py:220
Sparse Core Ops, SparseCore 0:
  23.3 47.4 all-gather.1
  137.2 20.3 reduce-scatter.1
